TPU v7x, 32 devices: a whole 2x2x4 slice. The times are simulated.
32 devices in a mesh: req: 2 (over x), seq: 16 (over z, y, core).
Axes of the slice: x: 2, y: 2, z: 4, core: 2. Of those that a mesh axis runs over, the one named last changes fastest.
Arguments:
- states: bfloat16 [4, 4, 4544], P(None, 'req', 'seq'), may hold values from -6 to 6
- kv_cache: bfloat16 [4, 8192, 128], P('req', 'seq'), may hold values from -48 to 48, as said below
- lengths: int32 [4], replicated, may hold values from 1 to 8188, as said below
- placement: int32 [4], replicated, may hold values from 0 to 3, each once
- norm_gain: bfloat16 [4544], replicated, may hold values from 0.25 to 1.75
- norm_bias: bfloat16 [4544], replicated, may hold values from -1.5 to 1.5
- w_query: bfloat16 [4544, 4544], P('req', 'seq'), may hold values from -0.09375 to 0.09375
- w_keyval: bfloat16 [4544, 128], P('req'), may hold values from -0.09375 to 0.09375
- w_out: bfloat16 [4544, 4544], P('seq', 'req'), may hold values from -0.09375 to 0.09375
- w_up: bfloat16 [4544, 18176], P('req', 'seq'), may hold values from -0.09375 to 0.09375
- w_down: bfloat16 [18176, 4544], P('seq', 'req'), may hold values from -0.046875 to 0.046875
Outputs:
- new_states: bfloat16 [4, 4, 4544], P(None, 'req', 'seq')
- new_cache: bfloat16 [4, 8192, 128], P('req', 'seq')
Inputs may be any that keep to these rules, and one draw needn't show every extreme that they name: Request r's cache holds its first lengths[r] positions; some request has exactly 8188. `kv_cache`: row i is the cache of request placement[i]; positions at or beyond that request's length hold arbitrary values. `placement`: each request is served by exactly one slot.
All inputs are finite; a program needn't handle non-finite values.
Results may differ from a plain program's by a relative error of at most 0.012.
The roundings to bfloat16 on the way count: a program that leaves them out, or rounds other values in their place, can miss the bound.
Values may be sent and summed in bfloat16 or wider, within the bound.
No kernel may reach another device: no remote copies, remote signals or barrier semaphores. Data moves between devices by JAX's collectives and lax.ppermute only.
A program may use at most 192 MiB of HBM per device.

v0:
```python
import jax
import jax.numpy as jnp
from jax import lax
from jax.sharding import PartitionSpec as P

EPSILON = 1e-05
NEGATIVE = -1e30
ALL = ("req", "seq")


def layer_norm(row_block, norm_gain, norm_bias):
    values = row_block.astype(jnp.float32)
    average = jnp.mean(values, axis=-1, keepdims=True)
    centered = values - average
    spread = jnp.mean(centered * centered, axis=-1, keepdims=True)
    scaled = centered * lax.rsqrt(spread + EPSILON)
    return (scaled * norm_gain.astype(jnp.float32) + norm_bias.astype(jnp.float32)).astype(
        jnp.bfloat16
    )


def rotate(vectors, positions):
    head_width = vectors.shape[-1]
    half_width = head_width // 2
    frequency = 10000.0 ** (-(jnp.arange(half_width, dtype=jnp.float32) * 2.0) / head_width)
    angles = positions.astype(jnp.float32)[:, None] * frequency[None, :]
    cosine = jnp.concatenate([jnp.cos(angles), jnp.cos(angles)], axis=-1)[:, None, :]
    sine_wave = jnp.concatenate([jnp.sin(angles), jnp.sin(angles)], axis=-1)[:, None, :]
    turned = jnp.concatenate([-vectors[..., half_width:], vectors[..., :half_width]], axis=-1)
    return vectors * cosine + turned * sine_wave


def shards(
    states,
    kv_cache,
    lengths,
    placement,
    norm_gain,
    norm_bias,
    w_query,
    w_keyval,
    w_out,
    w_up,
    w_down,
):
    steps = states.shape[0]
    group_rows = kv_cache.shape[0]
    seg_length = kv_cache.shape[1]
    head_width = kv_cache.shape[2] // 2
    model_width = norm_gain.shape[0]
    head_count = model_width // head_width
    slice_width = states.shape[2]
    part_width = w_query.shape[0]
    total = placement.shape[0]
    req_size = total // group_rows
    seq_size = model_width // slice_width
    rows = steps * total
    group_index = lax.axis_index("req")
    shard_index = lax.axis_index("seq")
    own_requests = lax.dynamic_slice_in_dim(placement, group_index * group_rows, group_rows, 0)
    slot_lengths = jnp.take(lengths, own_requests)
    step_offsets = jnp.arange(steps, dtype=jnp.int32)
    positions = slot_lengths[None, :] + step_offsets[:, None]
    every = lax.all_gather(states, ALL, axis=0, tiled=False)
    every = every.reshape(req_size, seq_size, steps, group_rows, slice_width)
    every = every.transpose(2, 0, 3, 1, 4).reshape(steps, total, model_width)
    current_all = jnp.take(every, placement, axis=1)
    normed = layer_norm(current_all.reshape(rows, model_width), norm_gain, norm_bias)
    normed_part = lax.dynamic_slice_in_dim(normed, group_index * part_width, part_width, 1)
    part_query = jnp.dot(normed_part, w_query, preferred_element_type=jnp.float32)
    part_keyval = jnp.dot(normed_part, w_keyval, preferred_element_type=jnp.float32)
    part_up = jnp.dot(normed_part, w_up, preferred_element_type=jnp.float32)
    first = lax.psum(jnp.concatenate([part_query, part_keyval, part_up], axis=1), "req")
    query_raw = first[:, :slice_width].astype(jnp.bfloat16).reshape(steps, total, slice_width)
    keyval = first[:, slice_width : slice_width + 2 * head_width].reshape(
        steps, total, 2 * head_width
    )
    up_part = first[:, slice_width + 2 * head_width :]
    own_query = lax.dynamic_slice_in_dim(query_raw, group_index * group_rows, group_rows, 1)
    query_all = lax.all_gather(own_query, "seq", axis=2, tiled=True)
    flat_positions = positions.reshape(-1)
    query_rows = rotate(
        query_all.astype(jnp.float32).reshape(steps * group_rows, head_count, head_width),
        flat_positions,
    ).astype(jnp.bfloat16)
    own_keyval = lax.dynamic_slice_in_dim(keyval, group_index * group_rows, group_rows, 1)
    own_keyval = own_keyval.reshape(steps * group_rows, 2 * head_width)
    new_key = rotate(own_keyval[:, None, :head_width], flat_positions)[:, 0, :]
    new_entry = jnp.concatenate([new_key, own_keyval[:, head_width:]], axis=-1).astype(jnp.bfloat16)
    new_entry = new_entry.reshape(steps, group_rows, 2 * head_width)
    local_slots = jnp.arange(seg_length, dtype=jnp.int32)
    global_positions = shard_index * seg_length + local_slots
    cache_now = kv_cache
    for step_index in range(steps):
        write_mask = global_positions[None, :] == positions[step_index][:, None]
        cache_now = jnp.where(write_mask[:, :, None], new_entry[step_index][:, None, :], cache_now)
    key_rows = cache_now[:, :, :head_width]
    value_rows = cache_now[:, :, head_width:]
    query_heads = (
        query_rows.reshape(steps, group_rows, head_count, head_width)
        .transpose(1, 0, 2, 3)
        .reshape(group_rows, steps * head_count, head_width)
    )
    scores = jnp.einsum(
        "gqd,gsd->gqs", query_heads, key_rows, preferred_element_type=jnp.float32
    ) * head_width ** (-0.5)
    valid = global_positions[None, None, :] <= positions.T[:, :, None]
    valid = jnp.broadcast_to(
        valid[:, :, None, :], (group_rows, steps, head_count, seg_length)
    ).reshape(group_rows, steps * head_count, seg_length)
    local_peak = jnp.max(jnp.where(valid, scores, NEGATIVE), axis=-1)
    weights = jnp.where(valid, jnp.exp(scores - local_peak[:, :, None]), 0.0)
    local_total = jnp.sum(weights, axis=-1)
    local_weighted = jnp.einsum(
        "gqs,gsd->gqd", weights, value_rows, preferred_element_type=jnp.float32
    )
    peak_buffer = jnp.full((total, steps * head_count), NEGATIVE, jnp.float32)
    peak_buffer = lax.dynamic_update_slice_in_dim(
        peak_buffer, local_peak, group_index * group_rows, 0
    )
    peak = lax.pmax(peak_buffer, ALL)
    own_peak = lax.dynamic_slice_in_dim(peak, group_index * group_rows, group_rows, 0)
    scale = jnp.exp(local_peak - own_peak)
    packed = jnp.concatenate(
        [local_weighted * scale[:, :, None], (local_total * scale)[:, :, None]], axis=-1
    )
    packed_buffer = jnp.zeros((total, steps * head_count, head_width + 1), jnp.float32)
    packed_buffer = lax.dynamic_update_slice_in_dim(
        packed_buffer, packed, group_index * group_rows, 0
    )
    summed = lax.psum(packed_buffer, ALL)
    mixed = summed[:, :, :head_width] / summed[:, :, head_width:]
    mixed = (
        mixed.reshape(total, steps, model_width)
        .transpose(1, 0, 2)
        .reshape(rows, model_width)
        .astype(jnp.bfloat16)
    )
    mixed_part = lax.dynamic_slice_in_dim(mixed, shard_index * slice_width, slice_width, 1)
    hidden = jax.nn.gelu(up_part, approximate=False).astype(jnp.bfloat16)
    partial_sum = jnp.dot(mixed_part, w_out, preferred_element_type=jnp.float32) + jnp.dot(
        hidden, w_down, preferred_element_type=jnp.float32
    )
    out_buffer = jnp.zeros((rows, model_width), jnp.float32)
    out_buffer = lax.dynamic_update_slice_in_dim(
        out_buffer, partial_sum, group_index * part_width, 1
    )
    branch = lax.psum(out_buffer, ALL).reshape(steps, total, model_width)
    inverse = jnp.zeros((total,), jnp.int32).at[placement].set(jnp.arange(total, dtype=jnp.int32))
    own_inverse = lax.dynamic_slice_in_dim(inverse, group_index * group_rows, group_rows, 0)
    own_branch = jnp.take(branch, own_inverse, axis=1)
    own_branch = lax.dynamic_slice_in_dim(own_branch, shard_index * slice_width, slice_width, 2)
    new_states = (states.astype(jnp.float32) + own_branch).astype(jnp.bfloat16)
    return (new_states, cache_now)


def solution(mesh):
    in_specs = (
        P(None, "req", "seq"),
        P("req", "seq", None),
        P(),
        P(),
        P(),
        P(),
        P("req", "seq"),
        P("req", None),
        P("seq", "req"),
        P("req", "seq"),
        P("seq", "req"),
    )
    out_specs = (P(None, "req", "seq"), P("req", "seq", None))
    return jax.shard_map(shards, mesh=mesh, in_specs=in_specs, out_specs=out_specs, check_vma=False)
```

profile of v0, /device:TPU:8, one launch (start us, length us, event | category | flops | bytes accessed | tf_op | source)
XLA Modules:
  0.0 437.4 jit_solution(13402356280962080718)
XLA Ops:
  7.2 0.8 compare_select_fusion.2
  8.0 0.7 compare_and_fusion
  8.6 0.8 dynamic-slice.1
  9.4 0.8 dynamic-slice.2
  10.2 38.8 %all-gather = bf16[128,2,284]{2,1,0:T(2,128)(2,1)S(1)} all-gather(bf16[4,2,284]{2,1,0:T(2,128)(2,1)} %param.11), channel_id=2, replica_groups=mesh['req'=2,'seq'=16] {'req','seq'}, dimensions={0}, use_global_device_ids=true | all-gather | bytes 149952 | tf_op jit(solution)/shard_map/all_gather | solution.py:64
  49.0 0.3 reshape.348
  49.4 0.7 gather_fusion.1
  50.1 0.3 convert_reduce_fusion
  50.3 0.1 copy.70
  50.4 0.3 fusion.5
  50.7 0.1 copy.71
  50.8 0.1 rsqrt.12
  50.9 0.1 div.25
  51.1 0.1 broadcast_in_dim.144
  51.2 0.1 broadcast_select_fusion.1
  51.3 3.5 fusion.96
  54.8 0.3 fusion.94
  55.1 0.4 fusion.95
  55.5 0.8 concatenate.40
  56.5 0.6 gather_fusion
  57.4 0.1 multiply_cosine_fusion.1
  57.5 0.1 multiply_sine_fusion
  57.7 0.1 copy.81
  57.9 0.1 broadcast_in_dim.142
  58.0 0.2 reshape.346
  58.2 0.1 broadcast_compare_fusion.4
  58.3 19.3 %all-reduce.4.cloned.1.call-done = f32[16,1548]{1,0:T(8,128)} async-done(((f32[16,1548]{1,0:T(8,128)}), f32[16,1548]{1,0:T(8,128)}) %all-reduce.4.cloned.1.call-update) | async-done | bytes 99088 | tf_op jit(solution)/shard_map/psum | solution.py:73
  77.6 0.8 slice.99
  78.4 0.7 slice.124
  79.2 0.2 copy.88
  79.4 32.2 %all_gather.11 = bf16[4,2,4544]{0,1,2:T(2,128)(2,1)} all-gather(bf16[4,2,284]{0,1,2:T(2,128)(2,1)S(1)} %copy.88), channel_id=1, replica_groups=mesh['req'=2,'seq'=16] {'seq'}, dimensions={2}, use_global_device_ids=true | all-gather | bytes 77248 | tf_op jit(solution)/shard_map/all_gather | solution.py:80
  111.6 5.2 %copy.73 = bf16[4,2,4544]{2,0,1:T(4,128)(2,1)S(1)} copy(bf16[4,2,4544]{0,1,2:T(2,128)(2,1)} %all_gather.11) | data formatting | bytes 145408 | tf_op jit(solution)/shard_map/all_gather | solution.py:80
  116.8 0.2 reshape.351
  117.1 0.2 reshape.350
  117.6 0.1 fusion.98
  117.7 0.1 copy.89
  117.9 0.2 copy.78
  118.1 0.2 fusion.8
  118.2 0.2 copy.80
  118.4 0.1 reshape.352
  118.5 0.2 select_select_fusion
  118.8 0.5 select_reduce_fusion
  119.3 41.3 %pmax.7 = f32[4,284]{1,0:T(4,128)S(1)} all-reduce(f32[4,284]{1,0:T(4,128)S(1)} %constant_dynamic-update-slice_fusion.1), channel_id=1, replica_groups=mesh['req'=2,'seq'=16] {'req','seq'}, use_global_device_ids=true, to_apply=%region_5.6 | all-reduce | flops 1136 | bytes 9088 | tf_op jit(solution)/shard_map/pmax | solution.py:121
  160.6 0.4 fusion
  161.0 0.4 convolution_multiply_fusion.1
  161.5 0.2 copy.82
  161.7 0.8 copy-done.2
  162.6 0.6 scatter_custom_fusion
  163.2 129.3 %all-reduce.6.cloned.1.call-done = f32[4,284,65]{2,1,0:T(8,128)} async-done(((f32[4,284,65]{2,1,0:T(8,128)}), f32[4,284,65]{2,1,0:T(8,128)}) %all-reduce.6.cloned.1.call-update) | async-done | bytes 295376 | tf_op jit(solution)/shard_map/psum | solution.py:131
  292.5 1.5 slice_reduce_fusion
  294.0 1.3 fusion.1
  295.3 0.2 convert_element_type.69
  295.6 0.4 fusion.55
  296.0 0.2 copy-done.6
  296.2 3.4 convolution_add_fusion
  299.7 1.3 dynamic_update_slice.11
  301.0 0.1 reshape.355
  301.1 0.8 copy.84
  301.9 0.1 compare_and_fusion.1
  302.0 0.8 copy.86
  302.9 125.7 %all-reduce.8.cloned.1.call-done = f32[4,4,4544]{2,0,1:T(4,128)} async-done(((f32[4,4,4544]{2,0,1:T(4,128)}), f32[4,4,4544]{2,0,1:T(4,128)}) %all-reduce.8.cloned.1.call-update) | async-done | bytes 290832 | tf_op jit(solution)/shard_map/psum | solution.py:148
  428.5 1.6 gather_fusion.2
  430.1 0.1 fusion.54
  430.2 0.6 copy.85
  (65 shorter events, 1.6 us)
Async XLA Ops:
  7.2 288.4 %copy-start = (bf16[284,2272]{1,0:T(8,128)(2,1)S(1)}, bf16[284,2272]{1,0:T(8,128)(2,1)}, u32[]{:S(2)}) copy-start(bf16[284,2272]{1,0:T(8,128)(2,1)} %param.19) | copy-start | bytes 3871492
  7.2 70.4 %all-reduce.4.cloned.1.call-start = ((), (), s32[]{:S(2)}) async-start(), calls=%async_computation | async-start | bytes 212992 | tf_op jit(solution)/shard_map/psum | solution.py:73
  51.3 3.5 copy-start.4
  51.3 3.8 copy-start.3
  54.8 1.6 copy-start.8
  54.8 1.7 copy-start.1
  55.1 2.6 copy-start.5
  56.3 236.2 %all-reduce.6.cloned.1.call-start = ((), (), s32[]{:S(2)}) async-start(), calls=%async_computation.1 | async-start | bytes 1179648 | tf_op jit(solution)/shard_map/psum | solution.py:131
  161.7 0.8 copy-start.2
  162.6 266.0 %all-reduce.8.cloned.1.call-start = ((), (), s32[]{:S(2)}) async-start(), calls=%async_computation.2 | async-start | bytes 589824 | tf_op jit(solution)/shard_map/psum | solution.py:148
  295.3 0.9 copy-start.6
  301.0 129.2 %copy-start.7 = (bf16[4,2,284]{2,1,0:T(2,128)(2,1)S(1)}, bf16[4,2,284]{2,1,0:T(2,128)(2,1)}, u32[]{:S(2)}) copy-start(bf16[4,2,284]{2,1,0:T(2,128)(2,1)} %param.11) | copy-start | bytes 13636
Sparse Core Ops, SparseCore 0:
  56.4 21.1 all-reduce.3
  162.7 129.7 all-reduce.5
  302.1 126.4 all-reduce.7
where the time goes:
time: 438 us; the launch traced here: 437 us
  waiting for transfers between devices  274 us (63%)
  blocking collectives  112 us (26%)
  local copies, waits for them, and re-layouts  22.3 us (5%)
  between operations  14.2 us (3%)
  matrix products  8.89 us (2%)
  other arithmetic  5.32 us (1%)
    psum x1, waiting for transfers between devices, shards(): summed = lax.psum(packed_buffer, ALL)  129 us
    psum x1, waiting for transfers between devices, shards(): branch = lax.psum(out_buffer, ALL).reshape(steps, total, model_width)  126 us
    pmax x1, blocking collectives, shards(): peak = lax.pmax(peak_buffer, ALL)  41.3 us
    all_gather x1, blocking collectives, shards(): every = lax.all_gather(states, ALL, axis=0, tiled=False)  38.8 us
    all_gather x1, blocking collectives, shards(): query_all = lax.all_gather(own_query, 'seq', axis=2, tiled=True)  32.2 us
    psum x1, waiting for transfers between devices, shards(): lax.psum(jnp.concatenate([part_query, part_keyval, part_up], axis=1), 'req')  19.3 us
  transfers between devices with their start and end apart: 3, of which 3 were waited for; matrix products, arithmetic and copies ran while one was open for 1% of the time, Pallas kernels for 0%

commit v1 on v0

--- a/solution.py
+++ b/solution.py
@@ -6,6 +6,18 @@
 EPSILON = 1e-05
 NEGATIVE = -1e30
 ALL = ("req", "seq")
+
+
+def gather_by_bits(value, axis, dim):
+    ways, here = (lax.axis_size(axis), lax.axis_index(axis))
+    grown, reach = (value, 1)
+    while reach < ways:
+        theirs = lax.ppermute(grown, axis, [(d, d ^ reach) for d in range(ways)])
+        mine_first = jnp.concatenate([grown, theirs], axis=dim)
+        theirs_first = jnp.concatenate([theirs, grown], axis=dim)
+        grown = jnp.where(here & reach == 0, mine_first, theirs_first)
+        reach = 2 * reach
+    return grown
 
 
 def layer_norm(row_block, norm_gain, norm_bias):
@@ -77,7 +89,7 @@
     )
     up_part = first[:, slice_width + 2 * head_width :]
     own_query = lax.dynamic_slice_in_dim(query_raw, group_index * group_rows, group_rows, 1)
-    query_all = lax.all_gather(own_query, "seq", axis=2, tiled=True)
+    query_all = gather_by_bits(own_query, "seq", 2)
     flat_positions = positions.reshape(-1)
     query_rows = rotate(
         query_all.astype(jnp.float32).reshape(steps * group_rows, head_count, head_width),

time: 438 us -> 412 us (0.941)
  blocking collectives: 112 us -> 78.7 us
  waiting for transfers between devices: 274 us -> 282 us
  local copies, waits for them, and re-layouts: 22.3 us -> 16.9 us
  starting transfers between devices: 0.12 us -> 4.81 us
    all_gather x1 -> x0, blocking collectives: 32.2 us -> none  [shards(): query_all = lax.all_gather(own_query, 'seq', axis=2, tiled=True)]
    ppermute x0 -> x4, waiting for transfers between devices: none -> 8.58 us  [gather_by_bits(): theirs = lax.ppermute(grown, axis, [(d, d ^ reach) for d in range(ways)])]
    all_gather x1 -> x0, local copies, waits for them, and re-layouts: 5.18 us -> none  [shards(): query_all = lax.all_gather(own_query, 'seq', axis=2, tiled=True)]
    ppermute x0 -> x4, starting transfers between devices: none -> 4.69 us  [gather_by_bits(): theirs = lax.ppermute(grown, axis, [(d, d ^ reach) for d in range(ways)])]
  transfers between devices with their start and end apart: 3 -> 7, of which waited for: 3 -> 7; matrix products, arithmetic and copies ran while one was open for 1% -> 1% of each run, Pallas kernels for 0% -> 0%
where the time goes in v1:
time: 412 us; the launch traced here: 411 us
  waiting for transfers between devices  282 us (68%)
  blocking collectives  78.7 us (19%)
  local copies, waits for them, and re-layouts  16.9 us (4%)
  between operations  14.2 us (3%)
  matrix products  8.89 us (2%)
  other arithmetic  5.77 us (1%)
  starting transfers between devices  4.81 us (1%)
    psum x1, waiting for transfers between devices, shards(): summed = lax.psum(packed_buffer, ALL)  129 us
    psum x1, waiting for transfers between devices, shards(): branch = lax.psum(out_buffer, ALL).reshape(steps, total, model_width)  126 us
    pmax x1, blocking collectives, shards(): peak = lax.pmax(peak_buffer, ALL)  39.9 us
    all_gather x1, blocking collectives, shards(): every = lax.all_gather(states, ALL, axis=0, tiled=False)  38.8 us
    psum x1, waiting for transfers between devices, shards(): lax.psum(jnp.concatenate([part_query, part_keyval, part_up], axis=1), 'req')  19.2 us
    ppermute x4, waiting for transfers between devices, gather_by_bits(): theirs = lax.ppermute(grown, axis, [(d, d ^ reach) for d in range(ways)])  8.58 us
  transfers between devices with their start and end apart: 7, of which 7 were waited for; matrix products, arithmetic and copies ran while one was open for 1% of the time, Pallas kernels for 0%

profile of v1, /device:TPU:8, one launch (start us, length us, event | category | flops | bytes accessed | tf_op | source)
XLA Modules:
  0.0 411.4 jit_solution(739350821182533799)
XLA Ops:
  7.2 0.8 compare_select_fusion.2
  8.0 0.7 compare_and_fusion
  8.6 0.8 dynamic-slice.1
  9.4 0.8 dynamic-slice.2
  10.2 38.8 %all-gather = bf16[128,2,284]{2,1,0:T(2,128)(2,1)S(1)} all-gather(bf16[4,2,284]{2,1,0:T(2,128)(2,1)} %param.11), channel_id=2, replica_groups=mesh['req'=2,'seq'=16] {'req','seq'}, dimensions={0}, use_global_device_ids=true | all-gather | bytes 149952 | tf_op jit(solution)/shard_map/all_gather | solution.py:76
  49.0 0.3 reshape.355
  49.4 0.7 gather_fusion.1
  50.1 0.3 convert_reduce_fusion
  50.3 0.1 copy.67
  50.4 0.3 fusion.5
  50.7 0.1 copy.68
  51.1 0.1 broadcast_in_dim.144
  51.3 3.5 fusion.97
  54.8 0.3 fusion.95
  55.1 0.4 fusion.96
  55.5 0.8 concatenate.64
  56.5 0.6 gather_fusion
  57.4 0.1 multiply_cosine_fusion.1
  57.5 0.1 multiply_sine_fusion
  57.7 0.1 copy.74
  58.0 0.2 reshape.353
  58.4 19.2 %all-reduce.4.cloned.1.call-done = f32[16,1548]{1,0:T(8,128)} async-done(((f32[16,1548]{1,0:T(8,128)}), f32[16,1548]{1,0:T(8,128)}) %all-reduce.4.cloned.1.call-update) | async-done | bytes 99088 | tf_op jit(solution)/shard_map/psum | solution.py:85
  77.6 0.8 slice.99
  78.5 0.7 slice.124
  79.5 1.0 collective-permute-done
  80.5 0.1 broadcast_select_fusion.5
  80.6 1.5 collective-permute-start.1
  82.2 2.1 collective-permute-done.1
  84.3 0.1 broadcast_select_fusion.4
  84.4 0.6 collective-permute-start.2
  85.0 3.2 collective-permute-done.2
  88.2 0.1 broadcast_select_fusion.3
  88.4 2.5 collective-permute-start.3
  90.8 0.2 select_select_fusion
  91.0 2.2 collective-permute-done.3
  93.3 0.2 fusion.14
  93.4 0.2 reshape.362
  93.7 0.2 reshape.361
  93.9 0.1 fusion.99
  94.0 0.1 copy.81
  94.2 0.2 copy.71
  94.4 0.2 fusion.8
  94.5 0.2 copy.73
  94.7 0.1 reshape.357
  94.8 0.5 select_reduce_fusion
  95.4 39.9 %pmax.7 = f32[4,284]{1,0:T(4,128)S(1)} all-reduce(f32[4,284]{1,0:T(4,128)S(1)} %constant_dynamic-update-slice_fusion.1), channel_id=1, replica_groups=mesh['req'=2,'seq'=16] {'req','seq'}, use_global_device_ids=true, to_apply=%region_5.6 | all-reduce | flops 1136 | bytes 9088 | tf_op jit(solution)/shard_map/pmax | solution.py:133
  135.3 0.4 fusion
  135.7 0.4 convolution_multiply_fusion.1
  136.2 0.2 copy.75
  136.4 0.8 copy-done.2
  137.3 0.6 scatter_custom_fusion
  137.9 128.6 %all-reduce.6.cloned.1.call-done = f32[4,284,65]{2,1,0:T(8,128)} async-done(((f32[4,284,65]{2,1,0:T(8,128)}), f32[4,284,65]{2,1,0:T(8,128)}) %all-reduce.6.cloned.1.call-update) | async-done | bytes 295376 | tf_op jit(solution)/shard_map/psum | solution.py:143
  266.5 1.5 slice_reduce_fusion
  268.0 1.3 fusion.1
  269.3 0.2 convert_element_type.82
  269.6 0.4 fusion.56
  270.0 0.2 copy-done.6
  270.2 3.4 convolution_add_fusion
  273.7 1.3 dynamic_update_slice.11
  275.1 0.8 copy.77
  276.0 0.8 copy.79
  276.9 125.7 %all-reduce.8.cloned.1.call-done = f32[4,4,4544]{2,0,1:T(4,128)} async-done(((f32[4,4,4544]{2,0,1:T(4,128)}), f32[4,4,4544]{2,0,1:T(4,128)}) %all-reduce.8.cloned.1.call-update) | async-done | bytes 290832 | tf_op jit(solution)/shard_map/psum | solution.py:160
  402.5 1.6 gather_fusion.2
  404.2 0.6 copy.78
  (73 shorter events, 2.3 us)
Async XLA Ops:
  7.2 262.5 %copy-start = (bf16[284,2272]{1,0:T(8,128)(2,1)S(1)}, bf16[284,2272]{1,0:T(8,128)(2,1)}, u32[]{:S(2)}) copy-start(bf16[284,2272]{1,0:T(8,128)(2,1)} %param.19) | copy-start | bytes 3871492
  7.2 70.4 %all-reduce.4.cloned.1.call-start = ((), (), s32[]{:S(2)}) async-start(), calls=%async_computation | async-start | bytes 212992 | tf_op jit(solution)/shard_map/psum | solution.py:85
  51.3 3.5 copy-start.4
  51.3 3.8 copy-start.3
  54.8 1.6 copy-start.8
  54.8 1.7 copy-start.1
  55.1 2.6 copy-start.5
  56.3 210.2 %all-reduce.6.cloned.1.call-start = ((), (), s32[]{:S(2)}) async-start(), calls=%async_computation.1 | async-start | bytes 1179648 | tf_op jit(solution)/shard_map/psum | solution.py:143
  79.2 1.2 collective-permute-start
  80.6 3.7 collective-permute-start.1
  84.4 3.8 collective-permute-start.2
  88.4 4.9 %collective-permute-start.3 = (bf16[4,2,2272]{2,1,0:T(2,128)(2,1)S(1)}, bf16[4,2,2272]{2,1,0:T(2,128)(2,1)S(1)}, u32[]{:S(2)}, u32[]{:S(2)}) collective-permute-start(bf16[4,2,2272]{2,1,0:T(2,128)(2,1)S(1)} %broadcast_select_fusion.3), channel_id=1, source_target_pairs={{0,8},{1,9},{2,10},{3,11},{4,12},{5,13},{6,14},{7,15},{8,0},{9,1},... | collective-permute-start | bytes 109064 | tf_op jit(solution)/shard_map/ppermute | solution.py:15
  136.4 0.8 copy-start.2
  137.3 265.3 %all-reduce.8.cloned.1.call-start = ((), (), s32[]{:S(2)}) async-start(), calls=%async_computation.2 | async-start | bytes 589824 | tf_op jit(solution)/shard_map/psum | solution.py:160
  269.3 0.9 copy-start.6
  275.0 129.2 %copy-start.7 = (bf16[4,2,284]{2,1,0:T(2,128)(2,1)S(1)}, bf16[4,2,284]{2,1,0:T(2,128)(2,1)}, u32[]{:S(2)}) copy-start(bf16[4,2,284]{2,1,0:T(2,128)(2,1)} %param.11) | copy-start | bytes 13636
Sparse Core Ops, SparseCore 0:
  56.4 21.1 all-reduce.3
  137.4 129.0 all-reduce.5
  276.1 126.4 all-reduce.7
